TPU v7x, 32 devices: a whole 2x2x4 slice. The times are simulated.
32 devices in a mesh: grp: 4 (over y, core), blk: 8 (over z, x).
Axes of the slice: x: 2, y: 2, z: 4, core: 2. Of those that a mesh axis runs over, the one named last changes fastest.
Arguments:
- fields: float32 [14, 512, 4096], P(None, 'grp', 'blk'), may hold values from -6 to 6
- react_rate: float32 [512, 4096], P('grp', 'blk'), may hold values from 0.05 to 0.8
- mix_matrix: float32 [14, 14], replicated, may hold values from -1.5 to 1.5
- activation: float32 [14], replicated, may hold values from 0.3 to 4
- inlet_ids: int32 [4, 4096], P(None, 'blk'), may hold values from 0 to 4095
- inlet_weights: float32 [4, 4096], P(None, 'blk'), may hold values from 0.1 to 0.45
- outlet_ids: int32 [4, 4096], P(None, 'blk'), may hold values from 0 to 4095
- outlet_weights: float32 [4, 4096], P(None, 'blk'), may hold values from 0.1 to 0.45
Outputs:
- advanced: float32 [14, 512, 4096], P(None, 'grp', 'blk')
Inputs may be any that keep to these rules, and one draw needn't show every extreme that they name: Every inlet_ids entry names a row of the combustor exit plane. Every outlet_ids entry names a row of the turbine inlet plane.
All inputs are finite; a program needn't handle non-finite values.
Results may differ from a plain program's by a relative error of at most 0.00005.
Values sent between devices are 32-bit elements; how exact they have to be, the bound alone decides.
No kernel may reach another device: no remote copies, remote signals or barrier semaphores. Data moves between devices by JAX's collectives and lax.ppermute only.
A program may use at most 128 MiB of HBM per device.

v0:
```python
import jax
import jax.numpy as jnp
from jax import lax
from jax.sharding import PartitionSpec as P

courant = 0.5
diffusion = 0.1
source_step = 0.5


def padded(cells, sides, width, closed):
    for axis, dim in sides:
        count = lax.axis_size(axis)
        ends = count if closed else count - 1
        head = lax.slice_in_dim(cells, 0, width, axis=dim)
        tail = lax.slice_in_dim(cells, cells.shape[dim] - width, cells.shape[dim], axis=dim)
        cells = jnp.concatenate(
            [
                lax.ppermute(tail, axis, [(i, (i + 1) % count) for i in range(ends)]),
                cells,
                lax.ppermute(head, axis, [((i + 1) % count, i) for i in range(ends)]),
            ],
            axis=dim,
        )
    return cells


def tendency(values, backward, forward, cycle_left, cycle_right, rates, mix_matrix, activation):
    heat = 1.0 + jax.nn.softplus(values[4])
    reaction = rates[None] * values * jnp.exp(-activation[:, None, None] / heat[None])
    source = jnp.einsum("fg,gxr->fxr", mix_matrix, reaction, precision=lax.Precision.HIGHEST)
    advect = -courant * (values - backward)
    spread = diffusion * (backward + forward + cycle_left + cycle_right - 4.0 * values)
    return advect + spread + source_step * source


def faces(values):
    axial_pad = padded(values, (("grp", 1),), 1, False)
    cycle_pad = padded(values, (("blk", 2),), 1, True)
    return (axial_pad, cycle_pad)


def shards(
    fields, react_rate, mix_matrix, activation, inlet_ids, inlet_weights, outlet_ids, outlet_weights
):
    group_count = lax.axis_size("grp")
    group_index = lax.axis_index("grp")
    at_turbine = group_index == group_count - 1
    at_exit = group_index == group_count - 2
    axial_pad, cycle_pad = faces(fields)
    low_row = axial_pad[:, 0, :]
    high_row = axial_pad[:, -1, :]
    donors = lax.all_gather(low_row, "blk", axis=1, tiled=True)
    row_count = donors.shape[1]
    inside = (inlet_ids >= 0) & (inlet_ids < row_count)
    picked = jnp.take(donors, jnp.clip(inlet_ids, 0, row_count - 1), axis=1)
    weight = jnp.where(inside, inlet_weights, 0.0)
    inlet_values = jnp.sum(picked * weight[None], axis=1)
    pressure = lax.all_gather(high_row[4], "blk", axis=0, tiled=True)
    back_pressure = jnp.sum(jnp.take(pressure, outlet_ids) * outlet_weights, axis=0)

    def rate_of(values, axial_pad, cycle_pad):
        last_layer = values[:, -1, :]
        exit_ghost = last_layer.at[4].set(back_pressure)
        low_ghost = jnp.where(at_turbine, inlet_values, axial_pad[:, 0, :])
        high_ghost = jnp.where(
            at_turbine, last_layer, jnp.where(at_exit, exit_ghost, axial_pad[:, -1, :])
        )
        backward = jnp.concatenate([low_ghost[:, None, :], values[:, :-1, :]], axis=1)
        forward = jnp.concatenate([values[:, 1:, :], high_ghost[:, None, :]], axis=1)
        return tendency(
            values,
            backward,
            forward,
            cycle_pad[:, :, :-2],
            cycle_pad[:, :, 2:],
            react_rate,
            mix_matrix,
            activation,
        )

    first_section = fields + rate_of(fields, axial_pad, cycle_pad)
    second_axial, second_cycle = faces(first_section)
    return 0.5 * (fields + first_section + rate_of(first_section, second_axial, second_cycle))


def solution(mesh):
    in_specs = (
        P(None, "grp", "blk"),
        P("grp", "blk"),
        P(),
        P(),
        P(None, "blk"),
        P(None, "blk"),
        P(None, "blk"),
        P(None, "blk"),
    )
    out_specs = P(None, "grp", "blk")
    return jax.shard_map(shards, mesh=mesh, in_specs=in_specs, out_specs=out_specs, check_vma=False)
```

profile of v0, /device:TPU:1, one launch (start us, length us, event | category | flops | bytes accessed | tf_op | source)
XLA Modules:
  0.0 159.8 jit_solution(1495912322812927714)
XLA Ops:
  0.0 1.8 %fusion.48 = (f32[14,128,1]{2,1,0:T(8,128)S(1)}, f32[14,128,1]{2,1,0:T(8,128)S(1)}) fusion(f32[14,128,512]{2,1,0:T(8,128)} %param.12), kind=kLoop, calls=%fused_computation.72 | loop fusion | bytes 28672 | tf_op jit(solution)/shard_map/slice | solution.py:16
  1.8 0.3 copy.67
  2.1 5.1 %collective-permute-start.3 = (f32[14,128,1]{1,2,0:T(1,128)S(1)}, f32[14,128,1]{1,2,0:T(1,128)S(1)}, u32[]{:S(2)}, u32[]{:S(2)}) collective-permute-start(f32[14,128,1]{1,2,0:T(1,128)S(1)} %copy.67), channel_id=1, source_target_pairs={{1,0},{2,1},{3,2},{4,3},{5,4},{6,5},{7,6},{0,7},{9,8},{10,9},{11,1... | collective-permute-start | bytes 21512 | tf_op jit(solution)/shard_map/ppermute | solution.py:21
  7.2 0.3 copy.66
  7.5 0.0 collective-permute-start.2
  7.5 4.2 %copy.58 = f32[14,128,512]{2,0,1:T(8,128)S(1)} copy(f32[14,128,512]{2,1,0:T(8,128)} %param.12) | data formatting | bytes 7340032 | tf_op args[0]
  11.8 4.0 %collective-permute-start = (f32[14,1,512]{2,0,1:T(8,128)S(1)}, f32[14,1,512]{2,0,1:T(8,128)S(1)}, u32[]{:S(2)}, u32[]{:S(2)}) collective-permute-start(f32[14,1,512]{2,0,1:T(8,128)S(1)} %get-tuple-element.36), channel_id=1, source_target_pairs={{0,8},{8,16},{16,24},{1,9},{9,17},{17,25},{2,10},{10,18},{18,26},{... | collective-permute-start | bytes 86024 | tf_op jit(solution)/shard_map/ppermute | solution.py:19
  15.8 1.9 %collective-permute-start.1 = (f32[14,1,512]{2,0,1:T(8,128)S(1)}, f32[14,1,512]{2,0,1:T(8,128)S(1)}, u32[]{:S(2)}, u32[]{:S(2)}) collective-permute-start(f32[14,1,512]{2,0,1:T(8,128)S(1)} %get-tuple-element.38), channel_id=1, source_target_pairs={{8,0},{16,8},{24,16},{9,1},{17,9},{25,17},{10,2},{18,10},{26,18},{... | collective-permute-start | bytes 86024 | tf_op jit(solution)/shard_map/ppermute | solution.py:21
  17.7 1.3 fusion.33
  19.0 0.0 copy-start.3
  19.0 0.0 copy-start.5
  19.0 0.0 copy-start.4
  19.0 0.0 copy-start.7
  19.0 4.3 %fusion.47 = (f32[14,127,512]{2,0,1:T(8,128)}, f32[14,127,512]{2,0,1:T(8,128)}) fusion(f32[14,128,512]{2,0,1:T(8,128)S(1)} %copy.58), kind=kLoop, calls=%fused_computation.71 | loop fusion | bytes 14565376 | tf_op jit(solution)/shard_map/slice | solution.py:69
  23.5 0.0 collective-permute-done.2
  23.6 1.5 copy.49
  25.1 0.0 collective-permute-done.3
  25.1 1.4 copy.53
  26.5 0.0 collective-permute-done.1
  26.5 21.7 %all-gather.1 = f32[1,1,4096]{2,0,1:T(1,128)S(1)} all-gather(f32[1,1,512]{2,0,1:T(1,128)S(1)} %slice.121), channel_id=3, replica_groups=mesh['grp'=4,'blk'=8] {'blk'}, dimensions={2}, use_global_device_ids=true | all-gather | bytes 18432 | tf_op jit(solution)/shard_map/all_gather | solution.py:59
  48.1 11.8 %gather_fusion.1 = f32[2048]{0:T(1024)S(1)} fusion(f32[4096]{0:T(1024)S(1)} %bitcast.52, s32[2048]{0:T(1024)S(1)} %broadcast_clamp_fusion), kind=kCustom, calls=%fused_computation.1 | custom fusion | bytes 24576 | tf_op jit(solution)/shard_map/jit(_take)/gather | solution.py:60
  59.9 0.0 collective-permute-done
  59.9 24.8 %all-gather = f32[14,1,4096]{2,0,1:T(8,128)S(1)} all-gather(f32[14,1,512]{2,0,1:T(8,128)S(1)} %collective-permute-done), channel_id=2, replica_groups=mesh['grp'=4,'blk'=8] {'blk'}, dimensions={2}, use_global_device_ids=true | all-gather | bytes 258048 | tf_op jit(solution)/shard_map/all_gather | solution.py:53
  84.7 0.6 copy.42
  85.4 5.5 %gather_fusion = f32[2048,14]{1,0:T(8,128)S(1)} fusion(f32[14,4096]{0,1:T(8,128)S(1)} %copy.42, s32[2048]{0:T(1024)S(1)} %broadcast_clamp_fusion.1), kind=kCustom, calls=%fused_computation | custom fusion | bytes 237568 | tf_op jit(solution)/shard_map/jit(_take)/gather | solution.py:56
  90.9 0.7 multiply_reduce_fusion
  91.6 0.1 copy.43
  91.7 0.7 multiply_reduce_fusion.1
  92.4 0.2 scatter.6
  92.7 0.8 fusion.38
  93.5 14.2 %fusion.19 = f32[14,128,512]{2,0,1:T(8,128)S(1)} fusion(f32[14,128,512]{2,0,1:T(8,128)} %copy-done.1, f32[14,128,1]{2,0,1:T(8,128)} %copy.53, f32[14,128,1]{2,0,1:T(8,128)} %copy.49, f32[14,1,512]{2,0,1:T(8,128)S(1)} %fusion.38, f32[14,127,512]{2,0,1:T(8,128)} %get-tuple-element.40, f32[14,127,512]{2,0,1:T(8,128)} %get-tuple-element.39, ...), kind=kOutput, calls=%fused_computation.24 | convolution fusion | flops 171573248 | bytes 15219528 | tf_op jit(solution)/shard_map/fg,gxr->fxr/dot_general | solution.py:31
  107.7 0.4 fusion.45
  108.1 4.3 %fusion.44 = (f32[14,127,512]{2,0,1:T(8,128)}, f32[14,127,512]{2,0,1:T(8,128)}) fusion(f32[14,128,512]{2,0,1:T(8,128)S(1)} %fusion.19), kind=kLoop, calls=%fused_computation.68 | loop fusion | bytes 14565376 | tf_op jit(solution)/shard_map/slice | solution.py:69
  112.5 14.1 %collective-permute-start.4 = (f32[14,1,512]{2,0,1:T(8,128)S(1)}, f32[14,1,512]{2,0,1:T(8,128)S(1)}, u32[]{:S(2)}, u32[]{:S(2)}) collective-permute-start(f32[14,1,512]{2,0,1:T(8,128)S(1)} %get-tuple-element.29), channel_id=1, source_target_pairs={{0,8},{8,16},{16,24},{1,9},{9,17},{17,25},{2,10},{10,18},{18,26},{... | collective-permute-start | bytes 86024 | tf_op jit(solution)/shard_map/ppermute | solution.py:19
  126.5 0.4 copy.59
  126.9 0.4 copy.61
  127.3 3.2 %collective-permute-start.7 = (f32[14,128,1]{1,2,0:T(1,128)S(1)}, f32[14,128,1]{1,2,0:T(1,128)S(1)}, u32[]{:S(2)}, u32[]{:S(2)}) collective-permute-start(f32[14,128,1]{1,2,0:T(1,128)S(1)} %copy.61), channel_id=1, source_target_pairs={{1,0},{2,1},{3,2},{4,3},{5,4},{6,5},{7,6},{0,7},{9,8},{10,9},{11,1... | collective-permute-start | bytes 21512 | tf_op jit(solution)/shard_map/ppermute | solution.py:21
  130.5 0.0 collective-permute-start.6
  130.5 2.9 %fusion.34 = f32[1,128,512]{2,0,1:T(1,128)S(1)} fusion(f32[14,128,512]{2,0,1:T(8,128)} %copy-done.2), kind=kLoop, calls=%fused_computation.43 | loop fusion | flops 458752 | bytes 524288 | tf_op jit(solution)/shard_map/add | solution.py:29
  133.4 0.1 scatter.9
  133.4 2.1 %collective-permute-start.5 = (f32[14,1,512]{2,0,1:T(8,128)S(1)}, f32[14,1,512]{2,0,1:T(8,128)S(1)}, u32[]{:S(2)}, u32[]{:S(2)}) collective-permute-start(f32[14,1,512]{2,0,1:T(8,128)S(1)} %get-tuple-element.31), channel_id=1, source_target_pairs={{8,0},{16,8},{24,16},{9,1},{17,9},{25,17},{10,2},{18,10},{26,18},{... | collective-permute-start | bytes 86024 | tf_op jit(solution)/shard_map/ppermute | solution.py:21
  135.6 0.1 collective-permute-done.6
  135.7 0.5 copy.60
  136.2 0.5 copy.62
  136.8 1.9 %collective-permute-done.5 = f32[14,1,512]{2,0,1:T(8,128)S(1)} collective-permute-done((f32[14,1,512]{2,0,1:T(8,128)S(1)}, f32[14,1,512]{2,0,1:T(8,128)S(1)}, u32[]{:S(2)}, u32[]{:S(2)}) %collective-permute-start.5) | collective-permute-done | bytes 28704 | tf_op jit(solution)/shard_map/ppermute | solution.py:21
  138.7 0.8 fusion.36
  139.4 16.4 %fusion.12 = f32[14,128,512]{2,0,1:T(8,128)S(1)} fusion(f32[14,128,1]{2,0,1:T(8,128)S(1)} %copy.62, f32[14,128,512]{2,0,1:T(8,128)} %copy-done.2, f32[14,128,1]{2,0,1:T(8,128)S(1)} %copy.60, f32[14,1,512]{2,0,1:T(8,128)S(1)} %fusion.36, f32[14,127,512]{2,0,1:T(8,128)} %get-tuple-element.33, f32[14,127,512]{2,0,1:T(8,128)} %get-tuple-element.32, ...), kind=kOutput, calls=%fused_computation.15 | convolution fusion | flops 173408256 | bytes 18889544 | tf_op jit(solution)/shard_map/fg,gxr->fxr/dot_general | solution.py:31
  155.8 4.0 %copy.63 = f32[14,128,512]{2,1,0:T(8,128)} copy(f32[14,128,512]{2,0,1:T(8,128)S(1)} %fusion.12) | data formatting | bytes 7340032 | tf_op jit(solution)/shard_map/mul | solution.py:84
  (31 shorter events, 0.2 us)
Async XLA Ops:
  0.0 93.5 %copy-start = (f32[14,14]{1,0:T(8,128)S(1)}, f32[14,14]{1,0:T(8,128)}, u32[]{:S(2)}) copy-start(f32[14,14]{1,0:T(8,128)} %param.14) | copy-start | bytes 2356
  2.1 22.9 %collective-permute-start.3 = (f32[14,128,1]{1,2,0:T(1,128)S(1)}, f32[14,128,1]{1,2,0:T(1,128)S(1)}, u32[]{:S(2)}, u32[]{:S(2)}) collective-permute-start(f32[14,128,1]{1,2,0:T(1,128)S(1)} %copy.67), channel_id=1, source_target_pairs={{1,0},{2,1},{3,2},{4,3},{5,4},{6,5},{7,6},{0,7},{9,8},{10,9},{11,1... | collective-permute-start | bytes 21512 | tf_op jit(solution)/shard_map/ppermute | solution.py:21
  7.5 16.0 %collective-permute-start.2 = (f32[14,128,1]{1,2,0:T(1,128)S(1)}, f32[14,128,1]{1,2,0:T(1,128)S(1)}, u32[]{:S(2)}, u32[]{:S(2)}) collective-permute-start(f32[14,128,1]{1,2,0:T(1,128)S(1)} %copy.66), channel_id=1, source_target_pairs={{0,1},{1,2},{2,3},{3,4},{4,5},{5,6},{6,7},{7,0},{8,9},{9,10},{10,1... | collective-permute-start | bytes 21512 | tf_op jit(solution)/shard_map/ppermute | solution.py:19
  11.7 11.6 %copy-start.1 = (f32[14,128,512]{2,0,1:T(8,128)}, f32[14,128,512]{2,0,1:T(8,128)S(1)}, u32[]{:S(2)}) copy-start(f32[14,128,512]{2,0,1:T(8,128)S(1)} %copy.58) | copy-start | bytes 11010052
  11.8 48.2 %collective-permute-start = (f32[14,1,512]{2,0,1:T(8,128)S(1)}, f32[14,1,512]{2,0,1:T(8,128)S(1)}, u32[]{:S(2)}, u32[]{:S(2)}) collective-permute-start(f32[14,1,512]{2,0,1:T(8,128)S(1)} %get-tuple-element.36), channel_id=1, source_target_pairs={{0,8},{8,16},{16,24},{1,9},{9,17},{17,25},{2,10},{10,18},{18,26},{... | collective-permute-start | bytes 86024 | tf_op jit(solution)/shard_map/ppermute | solution.py:19
  15.8 10.7 %collective-permute-start.1 = (f32[14,1,512]{2,0,1:T(8,128)S(1)}, f32[14,1,512]{2,0,1:T(8,128)S(1)}, u32[]{:S(2)}, u32[]{:S(2)}) collective-permute-start(f32[14,1,512]{2,0,1:T(8,128)S(1)} %get-tuple-element.38), channel_id=1, source_target_pairs={{8,0},{16,8},{24,16},{9,1},{17,9},{25,17},{10,2},{18,10},{26,18},{... | collective-permute-start | bytes 86024 | tf_op jit(solution)/shard_map/ppermute | solution.py:21
  19.0 4.4 %copy-start.3 = (s32[4,512]{1,0:T(4,128)S(1)}, s32[4,512]{1,0:T(4,128)}, u32[]{:S(2)}) copy-start(s32[4,512]{1,0:T(4,128)} %param.16) | copy-start | bytes 24580
  19.0 4.4 %copy-start.5 = (f32[4,512]{1,0:T(4,128)S(1)}, f32[4,512]{1,0:T(4,128)}, u32[]{:S(2)}) copy-start(f32[4,512]{1,0:T(4,128)} %param.17) | copy-start | bytes 24580
  19.0 4.4 %copy-start.4 = (s32[4,512]{1,0:T(4,128)S(1)}, s32[4,512]{1,0:T(4,128)}, u32[]{:S(2)}) copy-start(s32[4,512]{1,0:T(4,128)} %param.18) | copy-start | bytes 24580
  19.0 4.5 %copy-start.7 = (f32[14]{0:T(128)S(1)}, f32[14]{0:T(128)}, u32[]{:S(2)}) copy-start(f32[14]{0:T(128)} %param.15) | copy-start | bytes 172
  107.7 4.7 %copy-start.2 = (f32[14,128,512]{2,0,1:T(8,128)}, f32[14,128,512]{2,0,1:T(8,128)S(1)}, u32[]{:S(2)}) copy-start(f32[14,128,512]{2,0,1:T(8,128)S(1)} %fusion.19) | copy-start | bytes 11010052
  112.4 27.0 %copy-start.6 = (f32[128,512]{1,0:T(8,128)S(1)}, f32[128,512]{1,0:T(8,128)}, u32[]{:S(2)}) copy-start(f32[128,512]{1,0:T(8,128)} %param.13) | copy-start | bytes 786436
  112.5 24.3 %collective-permute-start.4 = (f32[14,1,512]{2,0,1:T(8,128)S(1)}, f32[14,1,512]{2,0,1:T(8,128)S(1)}, u32[]{:S(2)}, u32[]{:S(2)}) collective-permute-start(f32[14,1,512]{2,0,1:T(8,128)S(1)} %get-tuple-element.29), channel_id=1, source_target_pairs={{0,8},{8,16},{16,24},{1,9},{9,17},{17,25},{2,10},{10,18},{18,26},{... | collective-permute-start | bytes 86024 | tf_op jit(solution)/shard_map/ppermute | solution.py:19
  127.3 8.9 %collective-permute-start.7 = (f32[14,128,1]{1,2,0:T(1,128)S(1)}, f32[14,128,1]{1,2,0:T(1,128)S(1)}, u32[]{:S(2)}, u32[]{:S(2)}) collective-permute-start(f32[14,128,1]{1,2,0:T(1,128)S(1)} %copy.61), channel_id=1, source_target_pairs={{1,0},{2,1},{3,2},{4,3},{5,4},{6,5},{7,6},{0,7},{9,8},{10,9},{11,1... | collective-permute-start | bytes 21512 | tf_op jit(solution)/shard_map/ppermute | solution.py:21
  130.5 5.2 %collective-permute-start.6 = (f32[14,128,1]{1,2,0:T(1,128)S(1)}, f32[14,128,1]{1,2,0:T(1,128)S(1)}, u32[]{:S(2)}, u32[]{:S(2)}) collective-permute-start(f32[14,128,1]{1,2,0:T(1,128)S(1)} %copy.59), channel_id=1, source_target_pairs={{0,1},{1,2},{2,3},{3,4},{4,5},{5,6},{6,7},{7,0},{8,9},{9,10},{10,1... | collective-permute-start | bytes 21512 | tf_op jit(solution)/shard_map/ppermute | solution.py:19
  133.4 5.2 %collective-permute-start.5 = (f32[14,1,512]{2,0,1:T(8,128)S(1)}, f32[14,1,512]{2,0,1:T(8,128)S(1)}, u32[]{:S(2)}, u32[]{:S(2)}) collective-permute-start(f32[14,1,512]{2,0,1:T(8,128)S(1)} %get-tuple-element.31), channel_id=1, source_target_pairs={{8,0},{16,8},{24,16},{9,1},{17,9},{25,17},{10,2},{18,10},{26,18},{... | collective-permute-start | bytes 86024 | tf_op jit(solution)/shard_map/ppermute | solution.py:21
where the time goes:
time: 160 us
  blocking collectives  46.5 us (29%)
  local copies, waits for them, and re-layouts  42.7 us (27%)
  matrix products  30.6 us (19%)
  starting transfers between devices  30.4 us (19%)
  other arithmetic  7.22 us (5%)
  waiting for transfers between devices  1.97 us (1%)
    dot_general x2, matrix products, tendency(): jnp.einsum('fg,gxr->fxr', mix_matrix, reaction, precision=lax.Precision.H...  30.6 us
    all_gather x1, blocking collectives, shards(): donors = lax.all_gather(low_row, 'blk', axis=1, tiled=True)  24.8 us
    all_gather x1, blocking collectives, shards(): pressure = lax.all_gather(high_row[4], 'blk', axis=0, tiled=True)  21.7 us
    ppermute x4, starting transfers between devices, padded(): lax.ppermute(tail, axis, [(i, (i + 1) % count) for i in range(ends)])  18.1 us
    ppermute x4, starting transfers between devices, padded(): lax.ppermute(head, axis, [((i + 1) % count, i) for i in range(ends)])  12.3 us
    gather x2, local copies, waits for them, and re-layouts, shards(): jnp.take(pressure, outlet_ids) * outlet_weights  11.8 us
    slice x2, local copies, waits for them, and re-layouts, rate_of(): values[:, :-1, :]  8.64 us
    gather x1, local copies, waits for them, and re-layouts, shards(): picked = jnp.take(donors, jnp.clip(inlet_ids, 0, row_count - 1), axis=1)  5.48 us
  transfers between devices with their start and end apart: 8, of which 2 were waited for; matrix products, arithmetic and copies ran while one was open for 19% of the time, Pallas kernels for 0%

commit v1 on v0

--- a/solution.py
+++ b/solution.py
@@ -2,6 +2,7 @@
 import jax.numpy as jnp
 from jax import lax
 from jax.sharding import PartitionSpec as P
+from jax.lax import axis_index, axis_size, ppermute
 
 courant = 0.5
 diffusion = 0.1
@@ -50,7 +51,16 @@
     axial_pad, cycle_pad = faces(fields)
     low_row = axial_pad[:, 0, :]
     high_row = axial_pad[:, -1, :]
-    donors = lax.all_gather(low_row, "blk", axis=1, tiled=True)
+    g_now, kept_arr = (axis_size("blk"), axis_index("blk"))
+    donors, carry_in = (low_row, 1)
+    while carry_in < g_now:
+        e_next = ppermute(
+            donors, axis_name="blk", perm=[(dev, dev ^ carry_in) for dev in range(g_now)]
+        )
+        z2 = jnp.concatenate([donors, e_next], axis=1)
+        y2 = jnp.concatenate([e_next, donors], axis=1)
+        donors = jnp.where(kept_arr & carry_in == 0, z2, y2)
+        carry_in = 2 * carry_in
     row_count = donors.shape[1]
     inside = (inlet_ids >= 0) & (inlet_ids < row_count)
     picked = jnp.take(donors, jnp.clip(inlet_ids, 0, row_count - 1), axis=1)

time: 160 us -> 140 us (0.88)
  blocking collectives: 46.5 us -> 23.1 us
  waiting for transfers between devices: 1.97 us -> 9.83 us
  starting transfers between devices: 30.4 us -> 25.8 us
    all_gather x1 -> x0, blocking collectives: 24.8 us -> none  [shards(): donors = lax.all_gather(low_row, 'blk', axis=1, tiled=True)]
    ppermute x0 -> x3, waiting for transfers between devices: none -> 7.87 us  [shards(): ppermute(donors, axis_name='blk', perm=[(dev, dev ^ carry_in) for dev in...]
    ppermute x4, starting transfers between devices: 18.1 us -> 15.6 us  [padded(): lax.ppermute(tail, axis, [(i, (i + 1) % count) for i in range(ends)])]
    ppermute x4, starting transfers between devices: 12.3 us -> 9.91 us  [padded(): lax.ppermute(head, axis, [((i + 1) % count, i) for i in range(ends)])]
    unnamed x23 -> x25, local copies, waits for them, and re-layouts: 4.88 us -> 4.88 us
  transfers between devices with their start and end apart: 8 -> 11, of which waited for: 2 -> 3; matrix products, arithmetic and copies ran while one was open for 19% -> 22% of each run, Pallas kernels for 0% -> 0%
where the time goes in v1:
time: 140 us
  local copies, waits for them, and re-layouts  42.7 us (30%)
  matrix products  31.1 us (22%)
  starting transfers between devices  25.8 us (18%)
  blocking collectives  23.1 us (16%)
  waiting for transfers between devices  9.83 us (7%)
  other arithmetic  6.56 us (5%)
    dot_general x2, matrix products, tendency(): jnp.einsum('fg,gxr->fxr', mix_matrix, reaction, precision=lax.Precision.H...  31.1 us
    all_gather x1, blocking collectives, shards(): pressure = lax.all_gather(high_row[4], 'blk', axis=0, tiled=True)  23.1 us
    ppermute x4, starting transfers between devices, padded(): lax.ppermute(tail, axis, [(i, (i + 1) % count) for i in range(ends)])  15.6 us
    gather x2, local copies, waits for them, and re-layouts, shards(): jnp.take(pressure, outlet_ids) * outlet_weights  11.8 us
    ppermute x4, starting transfers between devices, padded(): lax.ppermute(head, axis, [((i + 1) % count, i) for i in range(ends)])  9.91 us
    slice x2, local copies, waits for them, and re-layouts, rate_of(): values[:, :-1, :]  8.63 us
    ppermute x3, waiting for transfers between devices, shards(): ppermute(donors, axis_name='blk', perm=[(dev, dev ^ carry_in) for dev in...  7.87 us
    gather x1, local copies, waits for them, and re-layouts, shards(): picked = jnp.take(donors, jnp.clip(inlet_ids, 0, row_count - 1), axis=1)  5.48 us
  transfers between devices with their start and end apart: 11, of which 3 were waited for; matrix products, arithmetic and copies ran while one was open for 22% of the time, Pallas kernels for 0%

profile of v1, /device:TPU:1, one launch (start us, length us, event | category | flops | bytes accessed | tf_op | source)
XLA Modules:
  0.0 139.6 jit_solution(6479627552937901393)
XLA Ops:
  0.0 1.8 %fusion.48 = (f32[14,128,1]{2,1,0:T(8,128)S(1)}, f32[14,128,1]{2,1,0:T(8,128)S(1)}) fusion(f32[14,128,512]{2,1,0:T(8,128)} %param.12), kind=kLoop, calls=%fused_computation.75 | loop fusion | bytes 28672 | tf_op jit(solution)/shard_map/slice | solution.py:17
  1.8 0.3 copy.67
  2.1 5.1 %collective-permute-start.6 = (f32[14,128,1]{1,2,0:T(1,128)S(1)}, f32[14,128,1]{1,2,0:T(1,128)S(1)}, u32[]{:S(2)}, u32[]{:S(2)}) collective-permute-start(f32[14,128,1]{1,2,0:T(1,128)S(1)} %copy.67), channel_id=1, source_target_pairs={{1,0},{2,1},{3,2},{4,3},{5,4},{6,5},{7,6},{0,7},{9,8},{10,9},{11,1... | collective-permute-start | bytes 21512 | tf_op jit(solution)/shard_map/ppermute | solution.py:22
  7.2 0.3 copy.66
  7.5 0.0 collective-permute-start.5
  7.5 4.2 %copy.58 = f32[14,128,512]{2,0,1:T(8,128)S(1)} copy(f32[14,128,512]{2,1,0:T(8,128)} %param.12) | data formatting | bytes 7340032 | tf_op args[0]
  11.8 4.0 %collective-permute-start = (f32[14,1,512]{2,0,1:T(8,128)S(1)}, f32[14,1,512]{2,0,1:T(8,128)S(1)}, u32[]{:S(2)}, u32[]{:S(2)}) collective-permute-start(f32[14,1,512]{2,0,1:T(8,128)S(1)} %get-tuple-element.36), channel_id=1, source_target_pairs={{0,8},{8,16},{16,24},{1,9},{9,17},{17,25},{2,10},{10,18},{18,26},{... | collective-permute-start | bytes 86024 | tf_op jit(solution)/shard_map/ppermute | solution.py:20
  15.8 1.9 %collective-permute-start.4 = (f32[14,1,512]{2,0,1:T(8,128)S(1)}, f32[14,1,512]{2,0,1:T(8,128)S(1)}, u32[]{:S(2)}, u32[]{:S(2)}) collective-permute-start(f32[14,1,512]{2,0,1:T(8,128)S(1)} %get-tuple-element.38), channel_id=1, source_target_pairs={{8,0},{16,8},{24,16},{9,1},{17,9},{25,17},{10,2},{18,10},{26,18},{... | collective-permute-start | bytes 86024 | tf_op jit(solution)/shard_map/ppermute | solution.py:22
  17.7 1.3 fusion.33
  19.0 0.0 copy-start.3
  19.0 0.0 copy-start.5
  19.0 0.0 copy-start.4
  19.0 0.0 copy-start.8
  19.0 4.3 %fusion.47 = (f32[14,127,512]{2,0,1:T(8,128)}, f32[14,127,512]{2,0,1:T(8,128)}) fusion(f32[14,128,512]{2,0,1:T(8,128)S(1)} %copy.58), kind=kLoop, calls=%fused_computation.74 | loop fusion | bytes 14565376 | tf_op jit(solution)/shard_map/slice | solution.py:79
  23.5 0.1 collective-permute-start.1
  23.6 0.0 collective-permute-done.5
  23.7 1.5 %copy.49 = f32[14,128,1]{2,0,1:T(8,128)} copy(f32[14,128,1]{1,2,0:T(1,128)S(1)} %collective-permute-done.5) | data formatting | bytes 14336 | tf_op jit(solution)/shard_map/ppermute | solution.py:20
  25.1 1.4 %copy.53 = f32[14,128,1]{2,0,1:T(8,128)} copy(f32[14,128,1]{1,2,0:T(1,128)S(1)} %collective-permute-done.6) | data formatting | bytes 14336 | tf_op jit(solution)/shard_map/ppermute | solution.py:22
  26.6 23.1 %all-gather = f32[1,1,4096]{2,0,1:T(1,128)S(1)} all-gather(f32[1,1,512]{2,0,1:T(1,128)S(1)} %slice.121), channel_id=2, replica_groups=mesh['grp'=4,'blk'=8] {'blk'}, dimensions={2}, use_global_device_ids=true | all-gather | bytes 18432 | tf_op jit(solution)/shard_map/all_gather | solution.py:69
  49.7 11.8 %gather_fusion.1 = f32[2048]{0:T(1024)S(1)} fusion(f32[4096]{0:T(1024)S(1)} %bitcast.52, s32[2048]{0:T(1024)S(1)} %broadcast_clamp_fusion), kind=kCustom, calls=%fused_computation.1 | custom fusion | bytes 24576 | tf_op jit(solution)/shard_map/jit(_take)/gather | solution.py:70
  61.5 0.1 collective-permute-start.2
  61.6 0.2 scatter.6
  61.9 2.8 %collective-permute-done.2 = f32[14,1024]{1,0:T(8,128)S(1)} collective-permute-done((f32[14,1024]{1,0:T(8,128)S(1)}, f32[14,1024]{1,0:T(8,128)S(1)}, u32[]{:S(2)}, u32[]{:S(2)}) %collective-permute-start.2) | collective-permute-done | bytes 57376 | tf_op jit(solution)/shard_map/ppermute | solution.py:57
  64.7 0.1 collective-permute-start.3
  64.8 0.8 fusion.38
  65.5 5.1 %collective-permute-done.3 = f32[14,2048]{1,0:T(8,128)S(1)} collective-permute-done((f32[14,2048]{1,0:T(8,128)S(1)}, f32[14,2048]{1,0:T(8,128)S(1)}, u32[]{:S(2)}, u32[]{:S(2)}) %collective-permute-start.3) | collective-permute-done | bytes 114720 | tf_op jit(solution)/shard_map/ppermute | solution.py:57
  70.6 0.6 copy.42
  71.3 5.5 %gather_fusion = f32[2048,14]{1,0:T(8,128)S(1)} fusion(f32[14,4096]{0,1:T(8,128)S(1)} %copy.42, s32[2048]{0:T(1024)S(1)} %broadcast_clamp_fusion.1), kind=kCustom, calls=%fused_computation | custom fusion | bytes 237568 | tf_op jit(solution)/shard_map/jit(_take)/gather | solution.py:66
  76.8 0.7 multiply_reduce_fusion
  77.5 0.1 copy.43
  77.6 0.0 copy-done
  77.6 14.5 %fusion.19 = f32[14,128,512]{2,0,1:T(8,128)S(1)} fusion(f32[14,128,512]{2,0,1:T(8,128)} %copy-done.1, f32[14,128,1]{2,0,1:T(8,128)} %copy.53, f32[14,128,1]{2,0,1:T(8,128)} %copy.49, f32[14,1,512]{2,0,1:T(8,128)S(1)} %fusion.38, f32[14,127,512]{2,0,1:T(8,128)} %get-tuple-element.40, f32[14,127,512]{2,0,1:T(8,128)} %get-tuple-element.39, ...), kind=kOutput, calls=%fused_computation.24 | convolution fusion | flops 171573248 | bytes 15219528 | tf_op jit(solution)/shard_map/fg,gxr->fxr/dot_general | solution.py:32
  92.2 0.4 fusion.45
  92.6 4.3 %fusion.44 = (f32[14,127,512]{2,0,1:T(8,128)}, f32[14,127,512]{2,0,1:T(8,128)}) fusion(f32[14,128,512]{2,0,1:T(8,128)S(1)} %fusion.19), kind=kLoop, calls=%fused_computation.71 | loop fusion | bytes 14565376 | tf_op jit(solution)/shard_map/slice | solution.py:79
  96.9 10.9 %collective-permute-start.7 = (f32[14,1,512]{2,0,1:T(8,128)S(1)}, f32[14,1,512]{2,0,1:T(8,128)S(1)}, u32[]{:S(2)}, u32[]{:S(2)}) collective-permute-start(f32[14,1,512]{2,0,1:T(8,128)S(1)} %get-tuple-element.29), channel_id=1, source_target_pairs={{0,8},{8,16},{16,24},{1,9},{9,17},{17,25},{2,10},{10,18},{18,26},{... | collective-permute-start | bytes 86024 | tf_op jit(solution)/shard_map/ppermute | solution.py:20
  107.8 0.4 copy.59
  108.2 0.4 copy.61
  108.6 0.8 collective-permute-start.10
  109.3 0.7 collective-permute-start.9
  110.0 2.9 %fusion.34 = f32[1,128,512]{2,0,1:T(1,128)S(1)} fusion(f32[14,128,512]{2,0,1:T(8,128)} %copy-done.2), kind=kLoop, calls=%fused_computation.43 | loop fusion | flops 458752 | bytes 524288 | tf_op jit(solution)/shard_map/add | solution.py:30
  112.9 0.1 scatter.9
  113.0 2.1 %collective-permute-start.8 = (f32[14,1,512]{2,0,1:T(8,128)S(1)}, f32[14,1,512]{2,0,1:T(8,128)S(1)}, u32[]{:S(2)}, u32[]{:S(2)}) collective-permute-start(f32[14,1,512]{2,0,1:T(8,128)S(1)} %get-tuple-element.31), channel_id=1, source_target_pairs={{8,0},{16,8},{24,16},{9,1},{17,9},{25,17},{10,2},{18,10},{26,18},{... | collective-permute-start | bytes 86024 | tf_op jit(solution)/shard_map/ppermute | solution.py:22
  115.2 0.5 copy.60
  115.7 0.5 copy.62
  116.3 1.9 %collective-permute-done.8 = f32[14,1,512]{2,0,1:T(8,128)S(1)} collective-permute-done((f32[14,1,512]{2,0,1:T(8,128)S(1)}, f32[14,1,512]{2,0,1:T(8,128)S(1)}, u32[]{:S(2)}, u32[]{:S(2)}) %collective-permute-start.8) | collective-permute-done | bytes 28704 | tf_op jit(solution)/shard_map/ppermute | solution.py:22
  118.2 0.8 fusion.36
  119.0 16.6 %fusion.12 = f32[14,128,512]{2,0,1:T(8,128)S(1)} fusion(f32[14,128,1]{2,0,1:T(8,128)S(1)} %copy.62, f32[14,128,512]{2,0,1:T(8,128)} %copy-done.2, f32[14,128,1]{2,0,1:T(8,128)S(1)} %copy.60, f32[14,1,512]{2,0,1:T(8,128)S(1)} %fusion.36, f32[14,127,512]{2,0,1:T(8,128)} %get-tuple-element.33, f32[14,127,512]{2,0,1:T(8,128)} %get-tuple-element.32, ...), kind=kOutput, calls=%fused_computation.15 | convolution fusion | flops 173408256 | bytes 18889544 | tf_op jit(solution)/shard_map/fg,gxr->fxr/dot_general | solution.py:32
  135.6 4.0 %copy.63 = f32[14,128,512]{2,1,0:T(8,128)} copy(f32[14,128,512]{2,0,1:T(8,128)S(1)} %fusion.12) | data formatting | bytes 7340032 | tf_op jit(solution)/shard_map/mul | solution.py:94
  (41 shorter events, 0.3 us)
Async XLA Ops:
  0.0 77.6 %copy-start = (f32[14,14]{1,0:T(8,128)S(1)}, f32[14,14]{1,0:T(8,128)}, u32[]{:S(2)}) copy-start(f32[14,14]{1,0:T(8,128)} %param.14) | copy-start | bytes 2356
  2.1 23.0 %collective-permute-start.6 = (f32[14,128,1]{1,2,0:T(1,128)S(1)}, f32[14,128,1]{1,2,0:T(1,128)S(1)}, u32[]{:S(2)}, u32[]{:S(2)}) collective-permute-start(f32[14,128,1]{1,2,0:T(1,128)S(1)} %copy.67), channel_id=1, source_target_pairs={{1,0},{2,1},{3,2},{4,3},{5,4},{6,5},{7,6},{0,7},{9,8},{10,9},{11,1... | collective-permute-start | bytes 21512 | tf_op jit(solution)/shard_map/ppermute | solution.py:22
  7.5 16.1 %collective-permute-start.5 = (f32[14,128,1]{1,2,0:T(1,128)S(1)}, f32[14,128,1]{1,2,0:T(1,128)S(1)}, u32[]{:S(2)}, u32[]{:S(2)}) collective-permute-start(f32[14,128,1]{1,2,0:T(1,128)S(1)} %copy.66), channel_id=1, source_target_pairs={{0,1},{1,2},{2,3},{3,4},{4,5},{5,6},{6,7},{7,0},{8,9},{9,10},{10,1... | collective-permute-start | bytes 21512 | tf_op jit(solution)/shard_map/ppermute | solution.py:20
  11.7 11.6 %copy-start.1 = (f32[14,128,512]{2,0,1:T(8,128)}, f32[14,128,512]{2,0,1:T(8,128)S(1)}, u32[]{:S(2)}) copy-start(f32[14,128,512]{2,0,1:T(8,128)S(1)} %copy.58) | copy-start | bytes 11010052
  11.8 11.7 %collective-permute-start = (f32[14,1,512]{2,0,1:T(8,128)S(1)}, f32[14,1,512]{2,0,1:T(8,128)S(1)}, u32[]{:S(2)}, u32[]{:S(2)}) collective-permute-start(f32[14,1,512]{2,0,1:T(8,128)S(1)} %get-tuple-element.36), channel_id=1, source_target_pairs={{0,8},{8,16},{16,24},{1,9},{9,17},{17,25},{2,10},{10,18},{18,26},{... | collective-permute-start | bytes 86024 | tf_op jit(solution)/shard_map/ppermute | solution.py:20
  15.8 10.8 %collective-permute-start.4 = (f32[14,1,512]{2,0,1:T(8,128)S(1)}, f32[14,1,512]{2,0,1:T(8,128)S(1)}, u32[]{:S(2)}, u32[]{:S(2)}) collective-permute-start(f32[14,1,512]{2,0,1:T(8,128)S(1)} %get-tuple-element.38), channel_id=1, source_target_pairs={{8,0},{16,8},{24,16},{9,1},{17,9},{25,17},{10,2},{18,10},{26,18},{... | collective-permute-start | bytes 86024 | tf_op jit(solution)/shard_map/ppermute | solution.py:22
  19.0 4.4 %copy-start.3 = (s32[4,512]{1,0:T(4,128)S(1)}, s32[4,512]{1,0:T(4,128)}, u32[]{:S(2)}) copy-start(s32[4,512]{1,0:T(4,128)} %param.16) | copy-start | bytes 24580
  19.0 4.4 %copy-start.5 = (f32[4,512]{1,0:T(4,128)S(1)}, f32[4,512]{1,0:T(4,128)}, u32[]{:S(2)}) copy-start(f32[4,512]{1,0:T(4,128)} %param.17) | copy-start | bytes 24580
  19.0 4.4 %copy-start.4 = (s32[4,512]{1,0:T(4,128)S(1)}, s32[4,512]{1,0:T(4,128)}, u32[]{:S(2)}) copy-start(s32[4,512]{1,0:T(4,128)} %param.18) | copy-start | bytes 24580
  19.0 4.6 %copy-start.8 = (f32[14]{0:T(128)S(1)}, f32[14]{0:T(128)}, u32[]{:S(2)}) copy-start(f32[14]{0:T(128)} %param.15) | copy-start | bytes 172
  23.5 38.0 %collective-permute-start.1 = (f32[14,512]{1,0:T(8,128)S(1)}, f32[14,512]{1,0:T(8,128)S(1)}, u32[]{:S(2)}, u32[]{:S(2)}) collective-permute-start(f32[14,512]{1,0:T(8,128)S(1)} %bitcast.56), channel_id=1, source_target_pairs={{0,1},{1,0},{2,3},{3,2},{4,5},{5,4},{6,7},{7,6},{8,9},{9,8},{10,11... | collective-permute-start | bytes 86024 | tf_op jit(solution)/shard_map/ppermute | solution.py:57
  49.7 11.9 %copy-start.6 = (f32[4,512]{1,0:T(4,128)S(1)}, f32[4,512]{1,0:T(4,128)}, u32[]{:S(2)}) copy-start(f32[4,512]{1,0:T(4,128)} %param.19) | copy-start | bytes 24580
  61.5 3.2 %collective-permute-start.2 = (f32[14,1024]{1,0:T(8,128)S(1)}, f32[14,1024]{1,0:T(8,128)S(1)}, u32[]{:S(2)}, u32[]{:S(2)}) collective-permute-start(f32[14,1024]{1,0:T(8,128)S(1)} %maximum_select_fusion.2), channel_id=1, source_target_pairs={{0,2},{1,3},{2,0},{3,1},{4,6},{5,7},{6,4},{7,5},{8,10},{9,11},{10,... | collective-permute-start | bytes 172040 | tf_op jit(solution)/shard_map/ppermute | solution.py:57
  64.7 5.9 %collective-permute-start.3 = (f32[14,2048]{1,0:T(8,128)S(1)}, f32[14,2048]{1,0:T(8,128)S(1)}, u32[]{:S(2)}, u32[]{:S(2)}) collective-permute-start(f32[14,2048]{1,0:T(8,128)S(1)} %maximum_select_fusion.1), channel_id=1, source_target_pairs={{0,4},{1,5},{2,6},{3,7},{4,0},{5,1},{6,2},{7,3},{8,12},{9,13},{10,... | collective-permute-start | bytes 344072 | tf_op jit(solution)/shard_map/ppermute | solution.py:57
  92.1 4.7 %copy-start.2 = (f32[14,128,512]{2,0,1:T(8,128)}, f32[14,128,512]{2,0,1:T(8,128)S(1)}, u32[]{:S(2)}) copy-start(f32[14,128,512]{2,0,1:T(8,128)S(1)} %fusion.19) | copy-start | bytes 11010052
  96.9 22.1 %copy-start.7 = (f32[128,512]{1,0:T(8,128)S(1)}, f32[128,512]{1,0:T(8,128)}, u32[]{:S(2)}) copy-start(f32[128,512]{1,0:T(8,128)} %param.13) | copy-start | bytes 786436
  96.9 19.4 %collective-permute-start.7 = (f32[14,1,512]{2,0,1:T(8,128)S(1)}, f32[14,1,512]{2,0,1:T(8,128)S(1)}, u32[]{:S(2)}, u32[]{:S(2)}) collective-permute-start(f32[14,1,512]{2,0,1:T(8,128)S(1)} %get-tuple-element.29), channel_id=1, source_target_pairs={{0,8},{8,16},{16,24},{1,9},{9,17},{17,25},{2,10},{10,18},{18,26},{... | collective-permute-start | bytes 86024 | tf_op jit(solution)/shard_map/ppermute | solution.py:20
  108.6 7.2 %collective-permute-start.10 = (f32[14,128,1]{1,2,0:T(1,128)S(1)}, f32[14,128,1]{1,2,0:T(1,128)S(1)}, u32[]{:S(2)}, u32[]{:S(2)}) collective-permute-start(f32[14,128,1]{1,2,0:T(1,128)S(1)} %copy.61), channel_id=1, source_target_pairs={{1,0},{2,1},{3,2},{4,3},{5,4},{6,5},{7,6},{0,7},{9,8},{10,9},{11,1... | collective-permute-start | bytes 21512 | tf_op jit(solution)/shard_map/ppermute | solution.py:22
  109.3 5.9 %collective-permute-start.9 = (f32[14,128,1]{1,2,0:T(1,128)S(1)}, f32[14,128,1]{1,2,0:T(1,128)S(1)}, u32[]{:S(2)}, u32[]{:S(2)}) collective-permute-start(f32[14,128,1]{1,2,0:T(1,128)S(1)} %copy.59), channel_id=1, source_target_pairs={{0,1},{1,2},{2,3},{3,4},{4,5},{5,6},{6,7},{7,0},{8,9},{9,10},{10,1... | collective-permute-start | bytes 21512 | tf_op jit(solution)/shard_map/ppermute | solution.py:20
  113.0 5.2 %collective-permute-start.8 = (f32[14,1,512]{2,0,1:T(8,128)S(1)}, f32[14,1,512]{2,0,1:T(8,128)S(1)}, u32[]{:S(2)}, u32[]{:S(2)}) collective-permute-start(f32[14,1,512]{2,0,1:T(8,128)S(1)} %get-tuple-element.31), channel_id=1, source_target_pairs={{8,0},{16,8},{24,16},{9,1},{17,9},{25,17},{10,2},{18,10},{26,18},{... | collective-permute-start | bytes 86024 | tf_op jit(solution)/shard_map/ppermute | solution.py:22
